TPU v7x, 512 devices: a whole 4x8x8 slice. The times are simulated.
512 devices in a mesh: row: 32 (over z, x), col: 16 (over y, core).
Axes of the slice: x: 4, y: 8, z: 8, core: 2. Of those that a mesh axis runs over, the one named last changes fastest.
Arguments:
- tokens: bfloat16 [16384, 5376], P('row', 'col'), may hold values from -240 to 240
- gain: float32 [5376], P('col'), may hold values from 0.1 to 1.9
- query_gain: float32 [128], replicated, may hold values from 0.1 to 1.9
- key_gain: float32 [128], replicated, may hold values from 0.1 to 1.9
- w_query: bfloat16 [5376, 4096], P('row', 'col'), may hold values from -0.21808224 to 0.21808224
- w_key: bfloat16 [5376, 2048], P('row', 'col'), may hold values from -0.21808224 to 0.21808224
- w_value: bfloat16 [5376, 2048], P('row', 'col'), may hold values from -0.21808224 to 0.21808224
Outputs:
- attended: bfloat16 [16384, 4096], P('row', 'col')
All inputs are finite; a program needn't handle non-finite values.
Results may differ from a plain program's by a relative error of at most 0.022.
Values may be sent and summed in bfloat16 or wider, within the bound.
No kernel may reach another device: no remote copies, remote signals or barrier semaphores. Data moves between devices by JAX's collectives and lax.ppermute only.
A program may use at most 64 MiB of HBM per device.

v0:
```python
import jax
import jax.numpy as jnp
from jax import lax
from jax.sharding import PartitionSpec as P

D = 5376
HD = 128
WINDOW = 1024
EPS = 1e-06
CLIP_FRACTION = 0.25
QUERY_SCALAR = 168.0
ROPE_BASE = 10000.0


def shifted(array, axis, by):
    peers = lax.axis_size(axis)
    pairs = [(i, i + by) for i in range(peers) if 0 <= i + by < peers]
    return lax.ppermute(array, axis, pairs)


def clip_with(weight, largest):
    bound = CLIP_FRACTION * largest
    return jnp.clip(weight.astype(jnp.float32), -bound, bound).astype(jnp.bfloat16)


def column_max(weight):
    return jnp.max(jnp.abs(weight.astype(jnp.float32)), axis=0)


def head_norm(values, head_gain):
    return values * lax.rsqrt(jnp.mean(values * values, axis=-1, keepdims=True) + EPS) * head_gain


def rotate(values, positions):
    half = values.shape[-1] // 2
    freqs = ROPE_BASE ** (-(jnp.arange(half, dtype=jnp.float32) * 2.0 / values.shape[-1]))
    angles = positions.astype(jnp.float32)[:, None] * freqs[None, :]
    cosine = jnp.cos(angles)[:, None, :]
    sine = jnp.sin(angles)[:, None, :]
    first = values[..., :half]
    second = values[..., half:]
    return jnp.concatenate(
        [first * cosine - second * sine, second * cosine + first * sine], axis=-1
    )


def local(tokens, gain, query_gain, key_gain, w_query, w_key, w_value):
    rows = tokens.shape[0]
    widened = tokens.astype(jnp.float32)
    squares = lax.psum(jnp.sum(widened * widened, axis=1), "col")
    inverse = lax.rsqrt(squares / D + EPS)[:, None]
    normed = (widened * inverse * gain[None, :]).astype(jnp.bfloat16)
    whole = lax.all_gather(normed, "col", axis=1, tiled=True)
    query_cols = w_query.shape[1]
    key_cols = w_key.shape[1]
    max_query, max_key, max_value = lax.pmax(
        (column_max(w_query), column_max(w_key), column_max(w_value)), "row"
    )
    clip_query = clip_with(w_query, max_query)
    clip_key = clip_with(w_key, max_key)
    clip_value = clip_with(w_value, max_value)
    panels = (
        lax.all_gather(clip_query, "row", axis=0, tiled=True),
        lax.all_gather(clip_key, "row", axis=0, tiled=True),
        lax.all_gather(clip_value, "row", axis=0, tiled=True),
    )
    query, keys, values = tuple(
        (jnp.dot(whole, panel, preferred_element_type=jnp.float32) for panel in panels)
    )
    heads_local = query_cols // HD
    kv_local = key_cols // HD
    group = heads_local // kv_local
    positions = lax.axis_index("row") * rows + jnp.arange(rows, dtype=jnp.int32)
    query = rotate(head_norm(query.reshape(rows, heads_local, HD), query_gain), positions).astype(
        jnp.bfloat16
    )
    keys = rotate(head_norm(keys.reshape(rows, kv_local, HD), key_gain), positions).astype(
        jnp.bfloat16
    )
    values = values.reshape(rows, kv_local, HD).astype(jnp.bfloat16)
    blocks_back = WINDOW // rows
    earlier_keys = []
    earlier_values = []
    for offset in range(blocks_back, 0, -1):
        moved_keys, moved_values = shifted((keys, values), "row", offset)
        earlier_keys.append(moved_keys)
        earlier_values.append(moved_values)
    all_keys = jnp.concatenate(earlier_keys + [keys], axis=0)
    all_values = jnp.concatenate(earlier_values + [values], axis=0)
    key_pos = (
        positions[0] - blocks_back * rows + jnp.arange((blocks_back + 1) * rows, dtype=jnp.int32)
    )
    grouped = query.reshape(rows, kv_local, group, HD)
    scores = jnp.einsum(
        "tkgd,skd->kgts", grouped, all_keys, preferred_element_type=jnp.float32
    ) * QUERY_SCALAR ** (-0.5)
    distance = positions[:, None] - key_pos[None, :]
    allowed = (distance >= 0) & (distance < WINDOW) & (key_pos[None, :] >= 0)
    expo = jnp.where(allowed, jnp.exp(scores), 0.0)
    total = jnp.sum(expo, axis=-1, keepdims=True)
    probs = (expo / total).astype(jnp.bfloat16)
    output = jnp.einsum("kgts,skd->tkgd", probs, all_values, preferred_element_type=jnp.float32)
    return output.reshape(rows, query_cols).astype(jnp.bfloat16)


def solution(mesh):
    placed = (
        P("row", "col"),
        P("col"),
        P(),
        P(),
        P("row", "col"),
        P("row", "col"),
        P("row", "col"),
    )
    return jax.shard_map(
        local, mesh=mesh, in_specs=placed, out_specs=P("row", "col"), check_vma=False
    )
```

profile of v0, /device:TPU:8, one launch (start us, length us, event | category | flops | bytes accessed | tf_op | source)
XLA Modules:
  0.0 401.3 jit_solution(10856325609628339359)
XLA Ops:
  8.1 0.9 fusion.30
  9.1 80.9 %all-reduce = (f32[128]{0:T(128)S(1)}, f32[256]{0:T(256)S(1)}, f32[128]{0:T(128)S(1)}) all-reduce(f32[128]{0:T(128)S(1)} %fusion.40, f32[256]{0:T(256)S(1)} %fusion.30, f32[128]{0:T(128)S(1)} %fusion.37), channel_id=1, replica_groups=mesh['row'=32,'col'=16] {'row'}, use_global_device_ids=true, to_apply=%region_5.0 | all-reduce | flops 512 | bytes 4096 | tf_op jit(solution)/shard_map/pmax | solution.py:56
  89.9 1.4 fusion.42
  91.4 1.1 fusion.9
  92.5 21.1 %psum.7 = f32[512]{0:T(512)S(1)} all-reduce(f32[512]{0:T(512)S(1)} %fusion.9), channel_id=1, replica_groups=mesh['row'=32,'col'=16] {'col'}, use_global_device_ids=true, to_apply=%region_1.0 | all-reduce | flops 512 | bytes 4096 | tf_op jit(solution)/shard_map/psum | solution.py:50
  113.6 1.9 fusion.11
  115.5 1.4 fusion.39
  117.0 1.6 fusion.32
  119.9 1.0 multiply_cosine_fusion
  120.8 1.2 fusion.4
  122.1 46.1 %all-gather.9.cloned.1.call-done = bf16[5376,128]{1,0:T(8,128)(2,1)} async-done(((bf16[168,128]{1,0:T(8,128)(2,1)}), bf16[5376,128]{1,0:T(8,128)(2,1)}) %all-gather.9.cloned.1.call-update) | async-done | bytes 1376272 | tf_op jit(solution)/shard_map/all_gather | solution.py:64
  168.1 45.8 %all-gather.5.cloned.1.call-done = bf16[512,5376]{0,1:T(8,128)(2,1)} async-done(((bf16[512,336]{0,1:T(8,128)(2,1)}), bf16[512,5376]{0,1:T(8,128)(2,1)}) %all-gather.5.cloned.1.call-update) | async-done | bytes 5505040 | tf_op jit(solution)/shard_map/all_gather | solution.py:53
  213.9 4.0 multiply_reduce_fusion.1
  218.6 3.4 collective-permute-start.3
  222.0 4.6 %collective-permute-start.2 = (bf16[512,1,128]{0,2,1:T(8,128)(2,1)S(1)}, bf16[512,1,128]{0,2,1:T(8,128)(2,1)S(1)}, u32[]{:S(2)}, u32[]{:S(2)}) collective-permute-start(bf16[512,1,128]{0,2,1:T(8,128)(2,1)S(1)} %pad_maximum_fusion), channel_id=1, source_target_pairs={{0,32},{16,48},{32,64},{48,80},{64,96},{80,112},{96,128},{112,144}... | collective-permute-start | bytes 393224 | tf_op jit(solution)/shard_map/ppermute | solution.py:18
  226.6 72.4 %all-gather.7.cloned.1.call-done = bf16[5376,128]{1,0:T(8,128)(2,1)} async-done(((bf16[168,128]{1,0:T(8,128)(2,1)}), bf16[5376,128]{1,0:T(8,128)(2,1)}) %all-gather.7.cloned.1.call-update) | async-done | bytes 1376272 | tf_op jit(solution)/shard_map/all_gather | solution.py:65
  299.0 4.6 %fusion.8 = bf16[512,1,128]{2,0,1:T(8,128)(2,1)S(1)} fusion(bf16[512,5376]{0,1:T(8,128)(2,1)} %all-gather.5.cloned.1.call-done, bf16[5376,128]{1,0:T(8,128)(2,1)} %all-gather.7.cloned.1.call-done), kind=kOutput, calls=%fused_computation.11 | convolution fusion | flops 704708608 | bytes 7012352 | tf_op jit(solution)/shard_map/dot_general | solution.py:68
  303.6 2.4 collective-permute-start.1
  306.0 4.7 %collective-permute-start = (bf16[512,1,128]{2,0,1:T(8,128)(2,1)S(1)}, bf16[512,1,128]{2,0,1:T(8,128)(2,1)S(1)}, u32[]{:S(2)}, u32[]{:S(2)}) collective-permute-start(bf16[512,1,128]{2,0,1:T(8,128)(2,1)S(1)} %fusion.8), channel_id=1, source_target_pairs={{0,32},{16,48},{32,64},{48,80},{64,96},{80,112},{96,128},{112,144}... | collective-permute-start | bytes 393224 | tf_op jit(solution)/shard_map/ppermute | solution.py:18
  310.7 73.5 %all-gather.11.cloned.1.call-done = bf16[5376,256]{1,0:T(8,128)(2,1)} async-done(((bf16[168,256]{1,0:T(8,128)(2,1)}), bf16[5376,256]{1,0:T(8,128)(2,1)}) %all-gather.11.cloned.1.call-update) | async-done | bytes 2752528 | tf_op jit(solution)/shard_map/all_gather | solution.py:63
  384.2 5.1 %multiply_reduce_fusion = (f32[512,2]{0,1:T(2,128)S(1)}, f32[512,256]{0,1:T(8,128)S(1)}) fusion(bf16[512,5376]{0,1:T(8,128)(2,1)} %all-gather.5.cloned.1.call-done, bf16[5376,256]{1,0:T(8,128)(2,1)} %all-gather.11.cloned.1.call-done), kind=kOutput, calls=%fused_computation.20 | convolution fusion | flops 1409547264 | bytes 8785920 | tf_op jit(solution)/shard_map/dot_general | solution.py:68
  390.0 1.9 fusion
  392.0 2.0 fusion.5
  394.0 0.8 copy.12
  (35 shorter events, 3.8 us)
Async XLA Ops:
  6.5 161.6 %all-gather.9.cloned.1.call-start = ((), (), s32[]{:S(2)}) async-start(), calls=%async_computation.2 | async-start | bytes 1419264 | tf_op jit(solution)/shard_map/all_gather | solution.py:64
  91.4 122.6 %all-gather.5.cloned.1.call-start = ((), (), s32[]{:S(2)}) async-start(), calls=%async_computation | async-start | bytes 5849088 | tf_op jit(solution)/shard_map/all_gather | solution.py:53
  113.6 104.3 %copy-start = (f32[128]{0:T(128)S(1)}, f32[128]{0:T(128)}, u32[]{:S(2)}) copy-start(f32[128]{0:T(128)} %param.10) | copy-start | bytes 1540
  115.4 183.6 %all-gather.7.cloned.1.call-start = ((), (), s32[]{:S(2)}) async-start(), calls=%async_computation.1 | async-start | bytes 1419264 | tf_op jit(solution)/shard_map/all_gather | solution.py:65
  116.9 267.3 %all-gather.11.cloned.1.call-start = ((), (), s32[]{:S(2)}) async-start(), calls=%async_computation.3 | async-start | bytes 2838528 | tf_op jit(solution)/shard_map/all_gather | solution.py:63
  218.6 171.4 %collective-permute-start.3 = (bf16[512,1,128]{0,2,1:T(8,128)(2,1)S(1)}, bf16[512,1,128]{0,2,1:T(8,128)(2,1)S(1)}, u32[]{:S(2)}, u32[]{:S(2)}) collective-permute-start(bf16[512,1,128]{0,2,1:T(8,128)(2,1)S(1)} %pad_maximum_fusion), channel_id=1, source_target_pairs={{0,16},{16,32},{32,48},{48,64},{64,80},{80,96},{96,112},{112,128},... | collective-permute-start | bytes 393224 | tf_op jit(solution)/shard_map/ppermute | solution.py:18
  222.0 168.0 %collective-permute-start.2 = (bf16[512,1,128]{0,2,1:T(8,128)(2,1)S(1)}, bf16[512,1,128]{0,2,1:T(8,128)(2,1)S(1)}, u32[]{:S(2)}, u32[]{:S(2)}) collective-permute-start(bf16[512,1,128]{0,2,1:T(8,128)(2,1)S(1)} %pad_maximum_fusion), channel_id=1, source_target_pairs={{0,32},{16,48},{32,64},{48,80},{64,96},{80,112},{96,128},{112,144}... | collective-permute-start | bytes 393224 | tf_op jit(solution)/shard_map/ppermute | solution.py:18
  303.6 85.9 %copy-start.1 = (f32[128]{0:T(128)S(1)}, f32[128]{0:T(128)}, u32[]{:S(2)}) copy-start(f32[128]{0:T(128)} %param.9) | copy-start | bytes 1540
  303.6 88.3 %collective-permute-start.1 = (bf16[512,1,128]{2,0,1:T(8,128)(2,1)S(1)}, bf16[512,1,128]{2,0,1:T(8,128)(2,1)S(1)}, u32[]{:S(2)}, u32[]{:S(2)}) collective-permute-start(bf16[512,1,128]{2,0,1:T(8,128)(2,1)S(1)} %fusion.8), channel_id=1, source_target_pairs={{0,16},{16,32},{32,48},{48,64},{64,80},{80,96},{96,112},{112,128},... | collective-permute-start | bytes 393224 | tf_op jit(solution)/shard_map/ppermute | solution.py:18
  306.0 86.0 %collective-permute-start = (bf16[512,1,128]{2,0,1:T(8,128)(2,1)S(1)}, bf16[512,1,128]{2,0,1:T(8,128)(2,1)S(1)}, u32[]{:S(2)}, u32[]{:S(2)}) collective-permute-start(bf16[512,1,128]{2,0,1:T(8,128)(2,1)S(1)} %fusion.8), channel_id=1, source_target_pairs={{0,32},{16,48},{32,64},{48,80},{64,96},{80,112},{96,128},{112,144}... | collective-permute-start | bytes 393224 | tf_op jit(solution)/shard_map/ppermute | solution.py:18
Sparse Core Ops, SparseCore 0:
  91.5 76.6 all-gather.8
  170.2 43.6 all-gather.4
  217.1 81.8 all-gather.6
  302.0 82.1 all-gather.10
where the time goes:
time: 402 us; the launch traced here: 401 us
  waiting for transfers between devices  238 us (59%)
  blocking collectives  102 us (25%)
  matrix products  17.5 us (4%)
  starting transfers between devices  15.2 us (4%)
  between operations  14 us (3%)
  other arithmetic  13.2 us (3%)
    pmax x1, blocking collectives, local(): lax.pmax((column_max(w_query), column_max(w_key), column_max(w_value)), '...  80.9 us
    all_gather x1, waiting for transfers between devices, local(): lax.all_gather(clip_query, 'row', axis=0, tiled=True)  73.5 us
    all_gather x1, waiting for transfers between devices, local(): lax.all_gather(clip_value, 'row', axis=0, tiled=True)  72.4 us
    all_gather x1, waiting for transfers between devices, local(): lax.all_gather(clip_key, 'row', axis=0, tiled=True)  46.1 us
    all_gather x1, waiting for transfers between devices, local(): whole = lax.all_gather(normed, 'col', axis=1, tiled=True)  45.8 us
    psum x1, blocking collectives, local(): squares = lax.psum(jnp.sum(widened * widened, axis=1), 'col')  21.1 us
    ppermute x4, starting transfers between devices, shifted(): return lax.ppermute(array, axis, pairs)  15.1 us
    dot_general x3, matrix products, local(): jnp.dot(whole, panel, preferred_element_type=jnp.float32)  13.6 us
  transfers between devices with their start and end apart: 8, of which 4 were waited for; matrix products, arithmetic and copies ran while one was open for 6% of the time, Pallas kernels for 0%

commit v1 on v0

--- a/solution.py
+++ b/solution.py
@@ -50,7 +50,12 @@
     squares = lax.psum(jnp.sum(widened * widened, axis=1), "col")
     inverse = lax.rsqrt(squares / D + EPS)[:, None]
     normed = (widened * inverse * gain[None, :]).astype(jnp.bfloat16)
-    whole = lax.all_gather(normed, "col", axis=1, tiled=True)
+    ring = [normed]
+    for hop in range(15):
+        ring.append(lax.ppermute(ring[-1], "col", [(dev, (dev + 1) % 16) for dev in range(16)]))
+    whole = jnp.roll(
+        jnp.concatenate(ring[::-1], axis=1), (lax.axis_index("col") + 1) * ring[0].shape[1], axis=1
+    )
     query_cols = w_query.shape[1]
     key_cols = w_key.shape[1]
     max_query, max_key, max_value = lax.pmax(

time: 402 us -> 357 us (0.89)
  waiting for transfers between devices: 238 us -> 166 us
  local copies, waits for them, and re-layouts: 1.62 us -> 32.1 us
  starting transfers between devices: 15.2 us -> 7.51 us
    ppermute x0 -> x15, waiting for transfers between devices: none -> 105 us  [local(): lax.ppermute(ring[-1], 'col', [(dev, (dev + 1) % 16) for dev in range(16)])]
    all_gather x1, waiting for transfers between devices: 72.4 us -> 0.02 us  [local(): lax.all_gather(clip_value, 'row', axis=0, tiled=True)]
    all_gather x1, waiting for transfers between devices: 46.1 us -> 0.01 us  [local(): lax.all_gather(clip_key, 'row', axis=0, tiled=True)]
    all_gather x1 -> x0, waiting for transfers between devices: 45.8 us -> none  [local(): whole = lax.all_gather(normed, 'col', axis=1, tiled=True)]
    unnamed x4 -> x48, local copies, waits for them, and re-layouts: 0.01 us -> 30.5 us
    all_gather x1, waiting for transfers between devices: 73.5 us -> 61.1 us  [local(): lax.all_gather(clip_query, 'row', axis=0, tiled=True)]
    ppermute x4, starting transfers between devices: 15.1 us -> 7.03 us  [shifted(): return lax.ppermute(array, axis, pairs)]
  transfers between devices with their start and end apart: 8 -> 22, of which waited for: 4 -> 16; matrix products, arithmetic and copies ran while one was open for 6% -> 16% of each run, Pallas kernels for 0% -> 0%
where the time goes in v1:
time: 357 us
  waiting for transfers between devices  166 us (46%)
  blocking collectives  102 us (29%)
  local copies, waits for them, and re-layouts  32.1 us (9%)
  matrix products  19.4 us (5%)
  other arithmetic  15.8 us (4%)
  between operations  14.1 us (4%)
  starting transfers between devices  7.51 us (2%)
    ppermute x15, waiting for transfers between devices, local(): lax.ppermute(ring[-1], 'col', [(dev, (dev + 1) % 16) for dev in range(16)])  105 us
    pmax x1, blocking collectives, local(): lax.pmax((column_max(w_query), column_max(w_key), column_max(w_value)), '...  80.8 us
    all_gather x1, waiting for transfers between devices, local(): lax.all_gather(clip_query, 'row', axis=0, tiled=True)  61.1 us
    unnamed x48, local copies, waits for them, and re-layouts  30.5 us
    psum x1, blocking collectives, local(): squares = lax.psum(jnp.sum(widened * widened, axis=1), 'col')  21.1 us
    dot_general x3, matrix products, local(): jnp.dot(whole, panel, preferred_element_type=jnp.float32)  14.5 us
  transfers between devices with their start and end apart: 22, of which 16 were waited for; matrix products, arithmetic and copies ran while one was open for 16% of the time, Pallas kernels for 0%

profile of v1, /device:TPU:8, one launch (start us, length us, event | category | flops | bytes accessed | tf_op | source)
XLA Modules:
  0.0 356.6 jit_solution(9660375419039649520)
XLA Ops:
  9.1 80.8 %all-reduce = (f32[128]{0:T(128)S(1)}, f32[256]{0:T(256)S(1)}, f32[128]{0:T(128)S(1)}) all-reduce(f32[128]{0:T(128)S(1)} %fusion.51, f32[256]{0:T(256)S(1)} %fusion.41, f32[128]{0:T(128)S(1)} %fusion.48), channel_id=1, replica_groups=mesh['row'=32,'col'=16] {'row'}, use_global_device_ids=true, to_apply=%region_5.6 | all-reduce | flops 512 | bytes 4096 | tf_op jit(solution)/shard_map/pmax | solution.py:61
  92.5 21.1 %psum.7 = f32[512]{0:T(512)S(1)} all-reduce(f32[512]{0:T(512)S(1)} %fusion.20), channel_id=1, replica_groups=mesh['row'=32,'col'=16] {'col'}, use_global_device_ids=true, to_apply=%region_1.0 | all-reduce | flops 512 | bytes 4096 | tf_op jit(solution)/shard_map/psum | solution.py:50
  115.1 8.0 %collective-permute-done = bf16[512,336]{0,1:T(8,128)(2,1)S(1)} collective-permute-done((bf16[512,336]{0,1:T(8,128)(2,1)S(1)}, bf16[512,336]{0,1:T(8,128)(2,1)S(1)}, u32[]{:S(2)}, u32[]{:S(2)}) %collective-permute-start) | collective-permute-done | bytes 344096 | tf_op jit(solution)/shard_map/ppermute | solution.py:55
  123.1 6.7 %collective-permute-done.1 = bf16[512,336]{0,1:T(8,128)(2,1)S(1)} collective-permute-done((bf16[512,336]{0,1:T(8,128)(2,1)S(1)}, bf16[512,336]{0,1:T(8,128)(2,1)S(1)}, u32[]{:S(2)}, u32[]{:S(2)}) %collective-permute-start.1) | collective-permute-done | bytes 344096 | tf_op jit(solution)/shard_map/ppermute | solution.py:55
  129.8 6.7 %collective-permute-done.2 = bf16[512,336]{0,1:T(8,128)(2,1)S(1)} collective-permute-done((bf16[512,336]{0,1:T(8,128)(2,1)S(1)}, bf16[512,336]{0,1:T(8,128)(2,1)S(1)}, u32[]{:S(2)}, u32[]{:S(2)}) %collective-permute-start.2) | collective-permute-done | bytes 344096 | tf_op jit(solution)/shard_map/ppermute | solution.py:55
  136.4 6.7 %collective-permute-done.3 = bf16[512,336]{0,1:T(8,128)(2,1)S(1)} collective-permute-done((bf16[512,336]{0,1:T(8,128)(2,1)S(1)}, bf16[512,336]{0,1:T(8,128)(2,1)S(1)}, u32[]{:S(2)}, u32[]{:S(2)}) %collective-permute-start.3) | collective-permute-done | bytes 344096 | tf_op jit(solution)/shard_map/ppermute | solution.py:55
  144.6 5.2 %collective-permute-done.4 = bf16[512,336]{0,1:T(8,128)(2,1)S(1)} collective-permute-done((bf16[512,336]{0,1:T(8,128)(2,1)S(1)}, bf16[512,336]{0,1:T(8,128)(2,1)S(1)}, u32[]{:S(2)}, u32[]{:S(2)}) %collective-permute-start.4) | collective-permute-done | bytes 344096 | tf_op jit(solution)/shard_map/ppermute | solution.py:55
  149.8 6.7 %collective-permute-done.5 = bf16[512,336]{0,1:T(8,128)(2,1)S(1)} collective-permute-done((bf16[512,336]{0,1:T(8,128)(2,1)S(1)}, bf16[512,336]{0,1:T(8,128)(2,1)S(1)}, u32[]{:S(2)}, u32[]{:S(2)}) %collective-permute-start.5) | collective-permute-done | bytes 344096 | tf_op jit(solution)/shard_map/ppermute | solution.py:55
  156.5 7.4 %collective-permute-done.6 = bf16[512,336]{0,1:T(8,128)(2,1)S(1)} collective-permute-done((bf16[512,336]{0,1:T(8,128)(2,1)S(1)}, bf16[512,336]{0,1:T(8,128)(2,1)S(1)}, u32[]{:S(2)}, u32[]{:S(2)}) %collective-permute-start.6) | collective-permute-done | bytes 344096 | tf_op jit(solution)/shard_map/ppermute | solution.py:55
  163.8 7.9 %collective-permute-done.7 = bf16[512,336]{0,1:T(8,128)(2,1)S(1)} collective-permute-done((bf16[512,336]{0,1:T(8,128)(2,1)S(1)}, bf16[512,336]{0,1:T(8,128)(2,1)S(1)}, u32[]{:S(2)}, u32[]{:S(2)}) %collective-permute-start.7) | collective-permute-done | bytes 344096 | tf_op jit(solution)/shard_map/ppermute | solution.py:55
  171.7 7.9 %collective-permute-done.8 = bf16[512,336]{0,1:T(8,128)(2,1)S(1)} collective-permute-done((bf16[512,336]{0,1:T(8,128)(2,1)S(1)}, bf16[512,336]{0,1:T(8,128)(2,1)S(1)}, u32[]{:S(2)}, u32[]{:S(2)}) %collective-permute-start.8) | collective-permute-done | bytes 344096 | tf_op jit(solution)/shard_map/ppermute | solution.py:55
  179.6 7.9 %collective-permute-done.9 = bf16[512,336]{0,1:T(8,128)(2,1)S(1)} collective-permute-done((bf16[512,336]{0,1:T(8,128)(2,1)S(1)}, bf16[512,336]{0,1:T(8,128)(2,1)S(1)}, u32[]{:S(2)}, u32[]{:S(2)}) %collective-permute-start.9) | collective-permute-done | bytes 344096 | tf_op jit(solution)/shard_map/ppermute | solution.py:55
  188.2 8.0 %collective-permute-done.10 = bf16[512,336]{0,1:T(8,128)(2,1)} collective-permute-done((bf16[512,336]{0,1:T(8,128)(2,1)S(1)}, bf16[512,336]{0,1:T(8,128)(2,1)}, u32[]{:S(2)}, u32[]{:S(2)}) %collective-permute-start.10) | collective-permute-done | bytes 344096 | tf_op jit(solution)/shard_map/ppermute | solution.py:55
  197.8 6.6 %collective-permute-done.11 = bf16[512,336]{0,1:T(8,128)(2,1)} collective-permute-done((bf16[512,336]{0,1:T(8,128)(2,1)}, bf16[512,336]{0,1:T(8,128)(2,1)}, u32[]{:S(2)}, u32[]{:S(2)}) %collective-permute-start.11) | collective-permute-done | bytes 344096 | tf_op jit(solution)/shard_map/ppermute | solution.py:55
  205.7 6.9 %collective-permute-done.12 = bf16[512,336]{0,1:T(8,128)(2,1)} collective-permute-done((bf16[512,336]{0,1:T(8,128)(2,1)}, bf16[512,336]{0,1:T(8,128)(2,1)}, u32[]{:S(2)}, u32[]{:S(2)}) %collective-permute-start.12) | collective-permute-done | bytes 344096 | tf_op jit(solution)/shard_map/ppermute | solution.py:55
  214.6 6.2 %collective-permute-done.13 = bf16[512,336]{0,1:T(8,128)(2,1)S(1)} collective-permute-done((bf16[512,336]{0,1:T(8,128)(2,1)}, bf16[512,336]{0,1:T(8,128)(2,1)S(1)}, u32[]{:S(2)}, u32[]{:S(2)}) %collective-permute-start.13) | collective-permute-done | bytes 344096 | tf_op jit(solution)/shard_map/ppermute | solution.py:55
  222.6 6.0 %collective-permute-done.14 = bf16[512,336]{0,1:T(8,128)(2,1)S(1)} collective-permute-done((bf16[512,336]{0,1:T(8,128)(2,1)S(1)}, bf16[512,336]{0,1:T(8,128)(2,1)S(1)}, u32[]{:S(2)}, u32[]{:S(2)}) %collective-permute-start.14) | collective-permute-done | bytes 344096 | tf_op jit(solution)/shard_map/ppermute | solution.py:55
  260.1 4.6 %multiply_reduce_fusion.1 = (f32[512]{0:T(512)S(1)}, f32[512,128]{0,1:T(8,128)S(1)}) fusion(bf16[5376,128]{1,0:T(8,128)(2,1)} %all-gather.6.cloned.1.call-done, bf16[512,10752]{0,1:T(8,128)(2,1)} %constant_dynamic-update-slice_fusion, s32[]{:T(128)S(6)} %select_n.18), kind=kOutput, calls=%fused_computation.46 | convolution fusion | flops 704773632 | bytes 7145476 | tf_op jit(solution)/shard_map/dot_general | solution.py:73
  268.2 4.6 %fusion.17 = bf16[512,1,128]{2,0,1:T(8,128)(2,1)S(1)} fusion(bf16[5376,128]{1,0:T(8,128)(2,1)} %all-gather.4.cloned.1.call-done, bf16[512,10752]{0,1:T(8,128)(2,1)} %constant_dynamic-update-slice_fusion, s32[]{:T(128)S(6)} %select_n.18), kind=kOutput, calls=%fused_computation.17 | convolution fusion | flops 704708608 | bytes 7012356 | tf_op jit(solution)/shard_map/dot_general | solution.py:73
  274.4 2.7 collective-permute-start.16
  277.2 61.1 %all-gather.8.cloned.1.call-done = bf16[5376,256]{1,0:T(8,128)(2,1)} async-done(((bf16[168,256]{1,0:T(8,128)(2,1)}), bf16[5376,256]{1,0:T(8,128)(2,1)}) %all-gather.8.cloned.1.call-update) | async-done | bytes 2752528 | tf_op jit(solution)/shard_map/all_gather | solution.py:68
  338.3 5.3 %multiply_reduce_fusion = (f32[512,2]{0,1:T(2,128)S(1)}, f32[512,256]{0,1:T(8,128)S(1)}) fusion(bf16[5376,256]{1,0:T(8,128)(2,1)} %all-gather.8.cloned.1.call-done, bf16[512,10752]{0,1:T(8,128)(2,1)} %constant_dynamic-update-slice_fusion, s32[]{:T(128)S(6)} %select_n.18), kind=kOutput, calls=%fused_computation.26 | convolution fusion | flops 1409547264 | bytes 8785924 | tf_op jit(solution)/shard_map/dot_general | solution.py:73
  344.3 1.9 fusion
  346.3 2.9 fusion.11
  (108 shorter events, 52.7 us)
Async XLA Ops:
  6.5 237.5 %copy-start = (bf16[512,336]{0,1:T(8,128)(2,1)S(1)}, bf16[512,336]{0,1:T(8,128)(2,1)}, u32[]{:S(2)}) copy-start(bf16[512,336]{0,1:T(8,128)(2,1)} %param.7) | copy-start | bytes 1032196
  6.5 237.5 %copy-start.6 = (f32[336]{0:T(512)S(1)}, f32[336]{0:T(512)}, u32[]{:S(2)}) copy-start(f32[336]{0:T(512)} %param.8) | copy-start | bytes 4036
  6.5 253.6 %all-gather.6.cloned.1.call-start = ((), (), s32[]{:S(2)}) async-start(), calls=%async_computation.1 | async-start | bytes 1419264 | tf_op jit(solution)/shard_map/all_gather | solution.py:69
  91.4 176.8 %all-gather.4.cloned.1.call-start = ((), (), s32[]{:S(2)}) async-start(), calls=%async_computation | async-start | bytes 1419264 | tf_op jit(solution)/shard_map/all_gather | solution.py:70
  114.7 8.4 %collective-permute-start = (bf16[512,336]{0,1:T(8,128)(2,1)S(1)}, bf16[512,336]{0,1:T(8,128)(2,1)S(1)}, u32[]{:S(2)}, u32[]{:S(2)}) collective-permute-start(bf16[512,336]{0,1:T(8,128)(2,1)S(1)} %fusion.22), channel_id=1, source_target_pairs={{0,1},{1,2},{2,3},{3,4},{4,5},{5,6},{6,7},{7,8},{8,9},{9,10},{10,1... | collective-permute-start | bytes 1032200 | tf_op jit(solution)/shard_map/ppermute | solution.py:55
  123.1 6.7 %collective-permute-start.1 = (bf16[512,336]{0,1:T(8,128)(2,1)S(1)}, bf16[512,336]{0,1:T(8,128)(2,1)S(1)}, u32[]{:S(2)}, u32[]{:S(2)}) collective-permute-start(bf16[512,336]{0,1:T(8,128)(2,1)S(1)} %collective-permute-done), channel_id=1, source_target_pairs={{0,1},{1,2},{2,3},{3,4},{4,5},{5,6},{6,7},{7,8},{8,9},{9,10},{10,1... | collective-permute-start | bytes 1032200 | tf_op jit(solution)/shard_map/ppermute | solution.py:55
  129.8 6.7 %collective-permute-start.2 = (bf16[512,336]{0,1:T(8,128)(2,1)S(1)}, bf16[512,336]{0,1:T(8,128)(2,1)S(1)}, u32[]{:S(2)}, u32[]{:S(2)}) collective-permute-start(bf16[512,336]{0,1:T(8,128)(2,1)S(1)} %collective-permute-done.1), channel_id=1, source_target_pairs={{0,1},{1,2},{2,3},{3,4},{4,5},{5,6},{6,7},{7,8},{8,9},{9,10},{10,1... | collective-permute-start | bytes 1032200 | tf_op jit(solution)/shard_map/ppermute | solution.py:55
  136.4 6.7 %collective-permute-start.3 = (bf16[512,336]{0,1:T(8,128)(2,1)S(1)}, bf16[512,336]{0,1:T(8,128)(2,1)S(1)}, u32[]{:S(2)}, u32[]{:S(2)}) collective-permute-start(bf16[512,336]{0,1:T(8,128)(2,1)S(1)} %collective-permute-done.2), channel_id=1, source_target_pairs={{0,1},{1,2},{2,3},{3,4},{4,5},{5,6},{6,7},{7,8},{8,9},{9,10},{10,1... | collective-permute-start | bytes 1032200 | tf_op jit(solution)/shard_map/ppermute | solution.py:55
  143.1 6.7 %collective-permute-start.4 = (bf16[512,336]{0,1:T(8,128)(2,1)S(1)}, bf16[512,336]{0,1:T(8,128)(2,1)S(1)}, u32[]{:S(2)}, u32[]{:S(2)}) collective-permute-start(bf16[512,336]{0,1:T(8,128)(2,1)S(1)} %collective-permute-done.3), channel_id=1, source_target_pairs={{0,1},{1,2},{2,3},{3,4},{4,5},{5,6},{6,7},{7,8},{8,9},{9,10},{10,1... | collective-permute-start | bytes 1032200 | tf_op jit(solution)/shard_map/ppermute | solution.py:55
  144.6 193.7 %all-gather.8.cloned.1.call-start = ((), (), s32[]{:S(2)}) async-start(), calls=%async_computation.2 | async-start | bytes 2838528 | tf_op jit(solution)/shard_map/all_gather | solution.py:68
  149.8 6.7 %collective-permute-start.5 = (bf16[512,336]{0,1:T(8,128)(2,1)S(1)}, bf16[512,336]{0,1:T(8,128)(2,1)S(1)}, u32[]{:S(2)}, u32[]{:S(2)}) collective-permute-start(bf16[512,336]{0,1:T(8,128)(2,1)S(1)} %collective-permute-done.4), channel_id=1, source_target_pairs={{0,1},{1,2},{2,3},{3,4},{4,5},{5,6},{6,7},{7,8},{8,9},{9,10},{10,1... | collective-permute-start | bytes 1032200 | tf_op jit(solution)/shard_map/ppermute | solution.py:55
  156.5 7.4 %collective-permute-start.6 = (bf16[512,336]{0,1:T(8,128)(2,1)S(1)}, bf16[512,336]{0,1:T(8,128)(2,1)S(1)}, u32[]{:S(2)}, u32[]{:S(2)}) collective-permute-start(bf16[512,336]{0,1:T(8,128)(2,1)S(1)} %collective-permute-done.5), channel_id=1, source_target_pairs={{0,1},{1,2},{2,3},{3,4},{4,5},{5,6},{6,7},{7,8},{8,9},{9,10},{10,1... | collective-permute-start | bytes 1032200 | tf_op jit(solution)/shard_map/ppermute | solution.py:55
  163.8 7.9 %collective-permute-start.7 = (bf16[512,336]{0,1:T(8,128)(2,1)S(1)}, bf16[512,336]{0,1:T(8,128)(2,1)S(1)}, u32[]{:S(2)}, u32[]{:S(2)}) collective-permute-start(bf16[512,336]{0,1:T(8,128)(2,1)S(1)} %collective-permute-done.6), channel_id=1, source_target_pairs={{0,1},{1,2},{2,3},{3,4},{4,5},{5,6},{6,7},{7,8},{8,9},{9,10},{10,1... | collective-permute-start | bytes 1032200 | tf_op jit(solution)/shard_map/ppermute | solution.py:55
  171.7 7.9 %collective-permute-start.8 = (bf16[512,336]{0,1:T(8,128)(2,1)S(1)}, bf16[512,336]{0,1:T(8,128)(2,1)S(1)}, u32[]{:S(2)}, u32[]{:S(2)}) collective-permute-start(bf16[512,336]{0,1:T(8,128)(2,1)S(1)} %collective-permute-done.7), channel_id=1, source_target_pairs={{0,1},{1,2},{2,3},{3,4},{4,5},{5,6},{6,7},{7,8},{8,9},{9,10},{10,1... | collective-permute-start | bytes 1032200 | tf_op jit(solution)/shard_map/ppermute | solution.py:55
  179.6 7.9 %collective-permute-start.9 = (bf16[512,336]{0,1:T(8,128)(2,1)S(1)}, bf16[512,336]{0,1:T(8,128)(2,1)S(1)}, u32[]{:S(2)}, u32[]{:S(2)}) collective-permute-start(bf16[512,336]{0,1:T(8,128)(2,1)S(1)} %collective-permute-done.8), channel_id=1, source_target_pairs={{0,1},{1,2},{2,3},{3,4},{4,5},{5,6},{6,7},{7,8},{8,9},{9,10},{10,1... | collective-permute-start | bytes 1032200 | tf_op jit(solution)/shard_map/ppermute | solution.py:55
  188.2 8.0 %collective-permute-start.10 = (bf16[512,336]{0,1:T(8,128)(2,1)S(1)}, bf16[512,336]{0,1:T(8,128)(2,1)}, u32[]{:S(2)}, u32[]{:S(2)}) collective-permute-start(bf16[512,336]{0,1:T(8,128)(2,1)S(1)} %collective-permute-done.9), channel_id=1, source_target_pairs={{0,1},{1,2},{2,3},{3,4},{4,5},{5,6},{6,7},{7,8},{8,9},{9,10},{10,1... | collective-permute-start | bytes 1032200 | tf_op jit(solution)/shard_map/ppermute | solution.py:55
  196.2 8.2 %collective-permute-start.11 = (bf16[512,336]{0,1:T(8,128)(2,1)}, bf16[512,336]{0,1:T(8,128)(2,1)}, u32[]{:S(2)}, u32[]{:S(2)}) collective-permute-start(bf16[512,336]{0,1:T(8,128)(2,1)} %collective-permute-done.10), channel_id=1, source_target_pairs={{0,1},{1,2},{2,3},{3,4},{4,5},{5,6},{6,7},{7,8},{8,9},{9,10},{10,1... | collective-permute-start | bytes 1032200 | tf_op jit(solution)/shard_map/ppermute | solution.py:55
  204.4 8.2 %collective-permute-start.12 = (bf16[512,336]{0,1:T(8,128)(2,1)}, bf16[512,336]{0,1:T(8,128)(2,1)}, u32[]{:S(2)}, u32[]{:S(2)}) collective-permute-start(bf16[512,336]{0,1:T(8,128)(2,1)} %collective-permute-done.11), channel_id=1, source_target_pairs={{0,1},{1,2},{2,3},{3,4},{4,5},{5,6},{6,7},{7,8},{8,9},{9,10},{10,1... | collective-permute-start | bytes 1032200 | tf_op jit(solution)/shard_map/ppermute | solution.py:55
  212.6 8.1 %collective-permute-start.13 = (bf16[512,336]{0,1:T(8,128)(2,1)}, bf16[512,336]{0,1:T(8,128)(2,1)S(1)}, u32[]{:S(2)}, u32[]{:S(2)}) collective-permute-start(bf16[512,336]{0,1:T(8,128)(2,1)} %collective-permute-done.12), channel_id=1, source_target_pairs={{0,1},{1,2},{2,3},{3,4},{4,5},{5,6},{6,7},{7,8},{8,9},{9,10},{10,1... | collective-permute-start | bytes 1032200 | tf_op jit(solution)/shard_map/ppermute | solution.py:55
  220.7 7.9 %collective-permute-start.14 = (bf16[512,336]{0,1:T(8,128)(2,1)S(1)}, bf16[512,336]{0,1:T(8,128)(2,1)S(1)}, u32[]{:S(2)}, u32[]{:S(2)}) collective-permute-start(bf16[512,336]{0,1:T(8,128)(2,1)S(1)} %collective-permute-done.13), channel_id=1, source_target_pairs={{0,1},{1,2},{2,3},{3,4},{4,5},{5,6},{6,7},{7,8},{8,9},{9,10},{10,1... | collective-permute-start | bytes 1032200 | tf_op jit(solution)/shard_map/ppermute | solution.py:55
  265.5 78.8 %collective-permute-start.17 = (bf16[512,1,128]{0,2,1:T(8,128)(2,1)S(1)}, bf16[512,1,128]{0,2,1:T(8,128)(2,1)S(1)}, u32[]{:S(2)}, u32[]{:S(2)}) collective-permute-start(bf16[512,1,128]{0,2,1:T(8,128)(2,1)S(1)} %pad_maximum_fusion), channel_id=1, source_target_pairs={{0,32},{16,48},{32,64},{48,80},{64,96},{80,112},{96,128},{112,144}... | collective-permute-start | bytes 393224 | tf_op jit(solution)/shard_map/ppermute | solution.py:18
  266.9 77.4 %collective-permute-start.18 = (bf16[512,1,128]{0,2,1:T(8,128)(2,1)S(1)}, bf16[512,1,128]{0,2,1:T(8,128)(2,1)S(1)}, u32[]{:S(2)}, u32[]{:S(2)}) collective-permute-start(bf16[512,1,128]{0,2,1:T(8,128)(2,1)S(1)} %pad_maximum_fusion), channel_id=1, source_target_pairs={{0,16},{16,32},{32,48},{48,64},{64,80},{80,96},{96,112},{112,128},... | collective-permute-start | bytes 393224 | tf_op jit(solution)/shard_map/ppermute | solution.py:18
  272.9 73.4 %collective-permute-start.15 = (bf16[512,1,128]{2,0,1:T(8,128)(2,1)S(1)}, bf16[512,1,128]{2,0,1:T(8,128)(2,1)S(1)}, u32[]{:S(2)}, u32[]{:S(2)}) collective-permute-start(bf16[512,1,128]{2,0,1:T(8,128)(2,1)S(1)} %fusion.17), channel_id=1, source_target_pairs={{0,32},{16,48},{32,64},{48,80},{64,96},{80,112},{96,128},{112,144}... | collective-permute-start | bytes 393224 | tf_op jit(solution)/shard_map/ppermute | solution.py:18
  274.4 71.8 %collective-permute-start.16 = (bf16[512,1,128]{2,0,1:T(8,128)(2,1)S(1)}, bf16[512,1,128]{2,0,1:T(8,128)(2,1)}, u32[]{:S(2)}, u32[]{:S(2)}) collective-permute-start(bf16[512,1,128]{2,0,1:T(8,128)(2,1)S(1)} %fusion.17), channel_id=1, source_target_pairs={{0,16},{16,32},{32,48},{48,64},{64,80},{80,96},{96,112},{112,128},... | collective-permute-start | bytes 393224 | tf_op jit(solution)/shard_map/ppermute | solution.py:18
  (7 other events, 387.6 us)
Sparse Core Ops, SparseCore 0:
  91.5 76.6 all-gather.5
  171.4 80.0 all-gather.3
  254.7 83.5 all-gather.7
